TPU v7x, 32 devices: a whole 2x2x4 slice. The times are simulated.
32 devices in a mesh: blk: 8 (over y, x, core), head: 4 (over z).
Axes of the slice: x: 2, y: 2, z: 4, core: 2. Of those that a mesh axis runs over, the one named last changes fastest.
Arguments:
- query_matrix: bfloat16 [4096, 4096], P(('blk', 'head')), may hold values from -6 to 6
- key_matrix: bfloat16 [4096, 512], P(('blk', 'head')), may hold values from -6 to 6
- value_matrix: bfloat16 [4096, 512], P(('blk', 'head')), may hold values from -6 to 6
- output_cotangent: bfloat16 [4096, 4096], P(('blk', 'head')), may hold values from -6 to 6
- forward_output: bfloat16 [4096, 4096], P(('blk', 'head')), may hold values from -6 to 6
- doc_ids: int32 [4096], P(('blk', 'head')), may hold values from 0 to 31, never falling along the last dimension, each value on 1 to 2048 neighbouring positions
Outputs:
- query_grad: bfloat16 [4096, 4096], P(('blk', 'head'))
- key_gradient: bfloat16 [4096, 512], P(('blk', 'head'))
- value_gradient: bfloat16 [4096, 512], P(('blk', 'head'))
Inputs may be any that keep to these rules, and one draw needn't show every extreme that they name: `doc_ids`: document numbers never fall along the window; every document has 2048 tokens or fewer and one has exactly 2048.
All inputs are finite; a program needn't handle non-finite values.
Results may differ from a plain program's by a relative error of at most 0.0051.
Values may be sent and summed in bfloat16 or wider, within the bound.
No kernel may reach another device: no remote copies, remote signals or barrier semaphores. Data moves between devices by JAX's collectives and lax.ppermute only.
A program may use at most 64 MiB of HBM per device.

v0:
```python
import jax
import jax.numpy as jnp
from jax import lax
from jax.sharding import PartitionSpec as P

HEAD_WIDTH = 128
DOC_SPAN = 4
masked_score = -1e30


def shifted(block, axis, distance):
    devices = range(lax.axis_size(axis))
    route = [(i - distance, i) for i in devices if i - distance in devices]
    return lax.ppermute(block, axis, route)


def passed_along(block, axis, distance):
    devices = range(lax.axis_size(axis))
    route = [((i - distance) % len(devices), i) for i in devices]
    return lax.ppermute(block, axis, route)


def per_device(query_matrix, key_matrix, value_matrix, output_cotangent, forward_output, doc_ids):
    cycle_size = lax.axis_size("blk")
    head_ways = lax.axis_size("head")
    block_rows = query_matrix.shape[0] * head_ways
    query_heads = query_matrix.shape[1] // (HEAD_WIDTH * head_ways)
    kv_heads = key_matrix.shape[1] // (HEAD_WIDTH * head_ways)
    heads_per_group = query_heads // kv_heads
    logit_scale = HEAD_WIDTH ** (-0.5)
    query_local, grad_local, output_local, key_local, value_local = (
        lax.all_to_all(query_matrix, "head", split_axis=1, concat_axis=0, tiled=True),
        lax.all_to_all(output_cotangent, "head", split_axis=1, concat_axis=0, tiled=True),
        lax.all_to_all(forward_output, "head", split_axis=1, concat_axis=0, tiled=True),
        lax.all_to_all(key_matrix, "head", split_axis=1, concat_axis=0, tiled=True),
        lax.all_to_all(value_matrix, "head", split_axis=1, concat_axis=0, tiled=True),
    )
    all_segments = lax.all_gather(doc_ids, ("blk", "head"), axis=0, tiled=True)
    my_block = lax.axis_index("blk")
    query_tensor = query_local.reshape(block_rows, kv_heads, heads_per_group, HEAD_WIDTH)
    returned_grads = grad_local.reshape(block_rows, kv_heads, heads_per_group, HEAD_WIDTH)
    stored_output = output_local.reshape(block_rows, kv_heads, heads_per_group, HEAD_WIDTH)
    row_terms = jnp.sum(
        returned_grads.astype(jnp.float32) * stored_output.astype(jnp.float32), axis=-1
    ).transpose(1, 2, 0)[..., None]
    query_segment = lax.dynamic_slice_in_dim(all_segments, my_block * block_rows, block_rows, 0)
    query_position = my_block * block_rows + jnp.arange(block_rows, dtype=jnp.int32)
    first_segment = all_segments[my_block * block_rows]

    def shares_doc(anchor):
        last_segment = all_segments[jnp.maximum(anchor, 0) * block_rows + block_rows - 1]
        return (anchor == my_block) | (anchor >= 0) & (anchor < my_block) & (
            last_segment == first_segment
        )

    def block_scores(key_block, anchor):
        key_split = key_block.reshape(block_rows, kv_heads, HEAD_WIDTH)
        key_segment = lax.dynamic_slice_in_dim(
            all_segments, jnp.maximum(anchor, 0) * block_rows, block_rows, 0
        )
        key_position = anchor * block_rows + jnp.arange(block_rows, dtype=jnp.int32)
        allowed = (query_segment[:, None] == key_segment[None, :]) & (
            key_position[None, :] <= query_position[:, None]
        )
        scores = (
            jnp.einsum(
                "ighd,jgd->ghij", query_tensor, key_split, preferred_element_type=jnp.float32
            )
            * logit_scale
        )
        return (jnp.where(allowed, scores, masked_score), allowed)

    def add_stats(running, key_block, anchor):
        run_max, run_sum = running
        scores, allowed = block_scores(key_block, anchor)
        new_max = jnp.maximum(run_max, jnp.max(scores, axis=-1, keepdims=True))
        new_sum = run_sum * jnp.exp(run_max - new_max) + jnp.sum(
            jnp.where(allowed, jnp.exp(scores - new_max), 0.0), axis=-1, keepdims=True
        )
        return (new_max, new_sum)

    near_blocks = [(key_local, value_local, my_block, 0)]
    for distance in range(1, min(DOC_SPAN, cycle_size - 1) + 1):
        near_key, near_value = shifted((key_local, value_local), "blk", distance)
        near_blocks.append((near_key, near_value, my_block - distance, distance))
    start_max = jnp.full((kv_heads, heads_per_group, block_rows, 1), masked_score, jnp.float32)
    start_sum = jnp.zeros((kv_heads, heads_per_group, block_rows, 1), jnp.float32)
    running = (start_max, start_sum)
    for near_key, near_value, anchor, distance in near_blocks:
        running = lax.cond(
            shares_doc(anchor),
            lambda inner, kb=near_key, og=anchor: add_stats(inner, kb, og),
            lambda inner: inner,
            running,
        )
    run_max, run_sum = running
    log_total = run_max + jnp.log(run_sum)

    def block_grads(operands):
        key_block, value_block, anchor = operands
        scores, allowed = block_scores(key_block, anchor)
        key_split = key_block.reshape(block_rows, kv_heads, HEAD_WIDTH)
        value_split = value_block.reshape(block_rows, kv_heads, HEAD_WIDTH)
        probabilities = jnp.where(allowed, jnp.exp(scores - log_total), 0.0)
        prob_grad = jnp.einsum(
            "ighd,jgd->ghij", returned_grads, value_split, preferred_element_type=jnp.float32
        )
        score_grad = (probabilities * (prob_grad - row_terms)).astype(jnp.bfloat16)
        weights_half = probabilities.astype(jnp.bfloat16)
        value_part = jnp.einsum(
            "ghij,ighd->jgd", weights_half, returned_grads, preferred_element_type=jnp.float32
        )
        key_part = jnp.einsum(
            "ghij,ighd->jgd", score_grad, query_tensor, preferred_element_type=jnp.float32
        )
        query_part = jnp.einsum(
            "ghij,jgd->ighd", score_grad, key_split, preferred_element_type=jnp.float32
        )
        return (
            query_part.reshape(block_rows, query_heads * HEAD_WIDTH),
            key_part.reshape(block_rows, kv_heads * HEAD_WIDTH),
            value_part.reshape(block_rows, kv_heads * HEAD_WIDTH),
        )

    def empty_grads(operands):
        return (
            jnp.zeros((block_rows, query_heads * HEAD_WIDTH), jnp.float32),
            jnp.zeros((block_rows, kv_heads * HEAD_WIDTH), jnp.float32),
            jnp.zeros((block_rows, kv_heads * HEAD_WIDTH), jnp.float32),
        )

    def maybe_grads(key_block, value_block, anchor):
        return lax.cond(
            shares_doc(anchor), block_grads, empty_grads, (key_block, value_block, anchor)
        )

    def pass_grads(grad_pair):
        return passed_along((grad_pair[0], grad_pair[1]), "blk", -1)

    def turn_step(turn_index, carried):
        key_block, value_block, query_total, summed_key_grad, summed_value_grad = carried
        anchor = (my_block + turn_index) % cycle_size
        query_part, key_part, value_part = maybe_grads(key_block, value_block, anchor)
        summed_key_grad, summed_value_grad = pass_grads(
            (summed_key_grad + key_part, summed_value_grad + value_part)
        )
        key_block, value_block = passed_along((key_block, value_block), "blk", -1)
        return (
            key_block,
            value_block,
            query_total + query_part,
            summed_key_grad,
            summed_value_grad,
        )

    starting_state = (
        key_local,
        value_local,
        jnp.zeros((block_rows, query_heads * HEAD_WIDTH), jnp.float32),
        jnp.zeros((block_rows, kv_heads * HEAD_WIDTH), jnp.float32),
        jnp.zeros((block_rows, kv_heads * HEAD_WIDTH), jnp.float32),
    )
    key_block, value_block, query_total, summed_key_grad, summed_value_grad = lax.fori_loop(
        0, cycle_size - 1, turn_step, starting_state
    )
    anchor = (my_block + (cycle_size - 1)) % cycle_size
    query_part, key_part, value_part = maybe_grads(key_block, value_block, anchor)
    query_total = query_total + query_part
    summed_key_grad, summed_value_grad = pass_grads(
        (summed_key_grad + key_part, summed_value_grad + value_part)
    )
    query_grad = (query_total * logit_scale).astype(jnp.bfloat16)
    key_gradient = (summed_key_grad * logit_scale).astype(jnp.bfloat16)
    value_gradient = summed_value_grad.astype(jnp.bfloat16)
    return (
        lax.all_to_all(query_grad, "head", split_axis=0, concat_axis=1, tiled=True),
        lax.all_to_all(key_gradient, "head", split_axis=0, concat_axis=1, tiled=True),
        lax.all_to_all(value_gradient, "head", split_axis=0, concat_axis=1, tiled=True),
    )


def solution(mesh):
    return jax.shard_map(
        per_device,
        mesh=mesh,
        in_specs=(
            P(("blk", "head"), None),
            P(("blk", "head"), None),
            P(("blk", "head"), None),
            P(("blk", "head"), None),
            P(("blk", "head"), None),
            P(("blk", "head")),
        ),
        out_specs=(P(("blk", "head"), None), P(("blk", "head"), None), P(("blk", "head"), None)),
        check_vma=False,
    )
```

profile of v0, /device:TPU:6, one launch (start us, length us, event | category | flops | bytes accessed | tf_op | source)
XLA Modules:
  0.0 454.4 jit_solution(7301382656809553807)
XLA Ops:
  2.2 4.9 %all-to-all-start = ((bf16[128,4,128]{2,0,1:T(8,128)(2,1)}), bf16[128,4,128]{2,0,1:T(8,128)(2,1)}, u32[]{:S(2)}, u32[]{:S(2)}) async-start(bf16[128,4,128]{2,0,1:T(8,128)(2,1)} %copy_bitcast_fusion.4), calls=%async_computation | async-start | bytes 262144 | tf_op jit(solution)/shard_map/all_to_all | solution.py:35
  9.4 3.9 all-to-all-done
  13.3 3.5 all-to-all-start.2
  19.1 22.1 %all-to-all-done.2 = bf16[128,4,1024]{2,0,1:T(8,128)(2,1)S(1)} async-done(((bf16[128,4,1024]{2,0,1:T(8,128)(2,1)}), bf16[128,4,1024]{2,0,1:T(8,128)(2,1)S(1)}, u32[]{:S(2)}, u32[]{:S(2)}) %all-to-all-start.2) | async-done | bytes 1048608 | tf_op jit(solution)/shard_map/all_to_all | solution.py:32
  41.2 3.5 all-to-all-start.3
  45.8 24.1 %all-to-all-done.3 = bf16[128,4,1024]{2,0,1:T(8,128)(2,1)S(1)} async-done(((bf16[128,4,1024]{2,0,1:T(8,128)(2,1)}), bf16[128,4,1024]{2,0,1:T(8,128)(2,1)S(1)}, u32[]{:S(2)}, u32[]{:S(2)}) %all-to-all-start.3) | async-done | bytes 1048608 | tf_op jit(solution)/shard_map/all_to_all | solution.py:33
  69.9 4.2 all-to-all-start.4
  74.3 75.4 %all-gather = s32[32,1,128]{2,1,0:T(1,128)S(1)} all-gather(s32[1,1,128]{2,1,0:T(1,128)S(1)} %bitcast.369), channel_id=1, replica_groups=mesh['blk'=8,'head'=4] {'blk','head'}, dimensions={0}, use_global_device_ids=true | all-gather | bytes 16896 | tf_op jit(solution)/shard_map/all_gather | solution.py:38
  168.2 5.6 %all-to-all-start.1 = ((bf16[128,4,128]{2,0,1:T(8,128)(2,1)}), bf16[128,4,128]{2,0,1:T(8,128)(2,1)}, u32[]{:S(2)}, u32[]{:S(2)}) async-start(bf16[128,4,128]{2,0,1:T(8,128)(2,1)} %copy_bitcast_fusion.3), calls=%async_computation.1 | async-start | bytes 262144 | tf_op jit(solution)/shard_map/all_to_all | solution.py:36
  183.4 5.7 %conditional.6 = ((f32[1,8,512,1]{2,1,3,0:T(8,128)S(1)}, f32[1,8,512,1]{2,1,3,0:T(8,128)S(1)})) conditional(s32[]{:T(128)} %convert_element_type.80, (f32[1,8,512,1]{2,1,3,0:T(8,128)S(1)}, f32[1,8,512,1]{2,1,3,0:T(8,128)S(1)}) %tuple.89, (s32[512]{0:T(512)S(1)}, s32[]{:T(128)}, s32[4096]{0:T(1024)}, s32[512]{0:T(512)S(1)}, ...), branch_computations={%region_2.3_spmd, %region_3.6_spmd} | conditional | flops 554443264 | bytes 18970726 | solution.py:90
  191.6 188.0 %while.26 = (s32[]{:T(128)}, bf16[512,128]{0,1:T(8,128)(2,1)S(1)}, bf16[512,128]{1,0:T(8,128)(2,1)}, f32[512,1024]{0,1:T(8,128)}, f32[512,128]{1,0:T(8,128)}, /*...) while((s32[]{:T(128)}, bf16[512,128]{0,1:T(8,128)(2,1)S(1)}, ...), condition=%wide.region_22.23_spmd.clone, body=%wide.region_19.22_spmd.clone.sunk | while | flops 2711487488 | bytes 62722972 | solution.py:163
  192.2 18.7 %collective-permute-start = (bf16[512,128]{0,1:T(8,128)(2,1)}, bf16[512,128]{0,1:T(8,128)(2,1)S(1)}, u32[]{:S(2)}, u32[]{:S(2)}) collective-permute-start(bf16[512,128]{0,1:T(8,128)(2,1)} %copy.187), channel_id=1, source_target_pairs={{4,0},{8,4},{12,8},{16,12},{20,16},{24,20},{28,24},{0,28},{5,1},{9... | collective-permute-start | bytes 393224 | tf_op jit(solution)/shard_map/while/body/eval_jaxpr/ppermute | solution.py:20
  214.9 13.2 %conditional.13 = (f32[512,1024]{0,1:T(8,128)S(1)}, f32[512,128]{1,0:T(8,128)}, f32[512,128]{1,0:T(8,128)S(1)}) conditional(s32[]{:T(128)} %convert_element_type.114, () %tuple.152, (s32[512]{0:T(512)S(1)}, s32[]{:T(128)}, s32[4096]{0:T(1024)}, s32[]{:T(128)}, bf16[512,1,8,128]{3,0,2,1:T(8,128)(2,1)S(1)}, /*index=5*/bf16[512,128]{0,1:T(8,128)(2,1)}, ...), branch_computations={%region_20.20_spmd, %region_21.21_spmd} | conditional | flops 2710307840 | bytes 50137280 | solution.py:133
  220.4 4.2 fusion.29
  302.3 13.1 %collective-permute-start.3 = (f32[512,128]{1,0:T(8,128)}, f32[512,128]{1,0:T(8,128)S(1)}, u32[]{:S(2)}, u32[]{:S(2)}) collective-permute-start(f32[512,128]{1,0:T(8,128)} %add.386), channel_id=1, source_target_pairs={{4,0},{8,4},{12,8},{16,12},{20,16},{24,20},{28,24},{0,28},{5,1},{9... | collective-permute-start | bytes 786440 | tf_op jit(solution)/shard_map/while/body/eval_jaxpr/ppermute | solution.py:20
  331.8 12.2 %collective-permute-start.3 = (f32[512,128]{1,0:T(8,128)}, f32[512,128]{1,0:T(8,128)S(1)}, u32[]{:S(2)}, u32[]{:S(2)}) collective-permute-start(f32[512,128]{1,0:T(8,128)} %add.386), channel_id=1, source_target_pairs={{4,0},{8,4},{12,8},{16,12},{20,16},{24,20},{28,24},{0,28},{5,1},{9... | collective-permute-start | bytes 786440 | tf_op jit(solution)/shard_map/while/body/eval_jaxpr/ppermute | solution.py:20
  360.3 12.3 %collective-permute-start.3 = (f32[512,128]{1,0:T(8,128)}, f32[512,128]{1,0:T(8,128)S(1)}, u32[]{:S(2)}, u32[]{:S(2)}) collective-permute-start(f32[512,128]{1,0:T(8,128)} %add.386), channel_id=1, source_target_pairs={{4,0},{8,4},{12,8},{16,12},{20,16},{24,20},{28,24},{0,28},{5,1},{9... | collective-permute-start | bytes 786440 | tf_op jit(solution)/shard_map/while/body/eval_jaxpr/ppermute | solution.py:20
  379.6 16.7 %conditional.10 = (f32[512,1024]{0,1:T(8,128)}, f32[512,128]{1,0:T(8,128)}, f32[512,128]{1,0:T(8,128)}) conditional(s32[]{:T(128)} %convert_element_type.85, () %tuple.95, (s32[512]{0:T(512)S(1)}, s32[]{:T(128)}, s32[4096]{0:T(1024)}, s32[512]{0:T(512)S(1)}, bf16[512,1,8,128]{3,2,0,1:T(8,128)(2,1)}, /*index=5*/bf16[512,128]{0,1:T(8,128)(2,1)S(1)}, ...), branch_computations={%region_23.24_spmd, %region_24.25_spmd} | conditional | flops 2710307328 | bytes 54360276 | solution.py:133
  387.9 4.4 fusion.55
  400.7 4.2 collective-permute-done.9
  405.0 4.8 %all-to-all-start.7 = ((bf16[4,128,128]{2,1,0:T(8,128)(2,1)}), bf16[4,128,128]{2,1,0:T(8,128)(2,1)S(1)}, u32[]{:S(2)}, u32[]{:S(2)}) async-start(bf16[4,128,128]{2,1,0:T(8,128)(2,1)} %bitcast.98), calls=%async_computation.7 | async-start | bytes 262144 | tf_op jit(solution)/shard_map/all_to_all | solution.py:178
  410.5 5.5 %all-to-all-done.7 = bf16[4,128,128]{2,1,0:T(8,128)(2,1)S(1)} async-done(((bf16[4,128,128]{2,1,0:T(8,128)(2,1)}), bf16[4,128,128]{2,1,0:T(8,128)(2,1)S(1)}, u32[]{:S(2)}, u32[]{:S(2)}) %all-to-all-start.7) | async-done | bytes 131104 | tf_op jit(solution)/shard_map/all_to_all | solution.py:178
  425.2 3.5 all-to-all-start.5
  430.5 21.9 %all-to-all-done.5 = bf16[4,128,1024]{2,1,0:T(8,128)(2,1)S(1)} async-done(((bf16[4,128,1024]{2,1,0:T(8,128)(2,1)}), bf16[4,128,1024]{2,1,0:T(8,128)(2,1)S(1)}, u32[]{:S(2)}, u32[]{:S(2)}) %all-to-all-start.5) | async-done | bytes 1048608 | tf_op jit(solution)/shard_map/all_to_all | solution.py:176
  (253 shorter events, 191.8 us)
Async XLA Ops:
  13.3 28.0 %all-to-all-start.2 = ((bf16[128,4,1024]{2,0,1:T(8,128)(2,1)}), bf16[128,4,1024]{2,0,1:T(8,128)(2,1)S(1)}, u32[]{:S(2)}, u32[]{:S(2)}) async-start(bf16[128,4,1024]{2,0,1:T(8,128)(2,1)} %bitcast.326), calls=%async_computation.2 | async-start | bytes 2097152 | tf_op jit(solution)/shard_map/all_to_all | solution.py:32
  41.2 28.7 %all-to-all-start.3 = ((bf16[128,4,1024]{2,0,1:T(8,128)(2,1)}), bf16[128,4,1024]{2,0,1:T(8,128)(2,1)S(1)}, u32[]{:S(2)}, u32[]{:S(2)}) async-start(bf16[128,4,1024]{2,0,1:T(8,128)(2,1)} %bitcast.325), calls=%async_computation.3 | async-start | bytes 2097152 | tf_op jit(solution)/shard_map/all_to_all | solution.py:33
  69.9 98.3 %all-to-all-start.4 = ((bf16[128,4,1024]{2,0,1:T(8,128)(2,1)}), bf16[128,4,1024]{2,0,1:T(8,128)(2,1)}, u32[]{:S(2)}, u32[]{:S(2)}) async-start(bf16[128,4,1024]{2,0,1:T(8,128)(2,1)} %bitcast.324), calls=%async_computation.4 | async-start | bytes 2097152 | tf_op jit(solution)/shard_map/all_to_all | solution.py:34
  158.9 30.3 %collective-permute-start.7 = (bf16[512,128]{1,0:T(8,128)(2,1)}, bf16[512,128]{1,0:T(8,128)(2,1)}, u32[]{:S(2)}, u32[]{:S(2)}) collective-permute-start(bf16[512,128]{1,0:T(8,128)(2,1)} %bitcast.67), channel_id=1, source_target_pairs={{0,16},{4,20},{8,24},{12,28},{1,17},{5,21},{9,25},{13,29},{2,18},{... | collective-permute-start | bytes 393224 | tf_op jit(solution)/shard_map/ppermute | solution.py:14
  160.2 29.0 %collective-permute-start.6 = (bf16[512,128]{1,0:T(8,128)(2,1)}, bf16[512,128]{1,0:T(8,128)(2,1)}, u32[]{:S(2)}, u32[]{:S(2)}) collective-permute-start(bf16[512,128]{1,0:T(8,128)(2,1)} %bitcast.67), channel_id=1, source_target_pairs={{0,12},{4,16},{8,20},{12,24},{16,28},{1,13},{5,17},{9,21},{13,25},... | collective-permute-start | bytes 393224 | tf_op jit(solution)/shard_map/ppermute | solution.py:14
  161.5 27.5 %collective-permute-start.5 = (bf16[512,128]{1,0:T(8,128)(2,1)}, bf16[512,128]{1,0:T(8,128)(2,1)}, u32[]{:S(2)}, u32[]{:S(2)}) collective-permute-start(bf16[512,128]{1,0:T(8,128)(2,1)} %bitcast.67), channel_id=1, source_target_pairs={{0,8},{4,12},{8,16},{12,20},{16,24},{20,28},{1,9},{5,13},{9,17},{1... | collective-permute-start | bytes 393224 | tf_op jit(solution)/shard_map/ppermute | solution.py:14
  162.8 20.5 %collective-permute-start.4 = (bf16[512,128]{1,0:T(8,128)(2,1)}, bf16[512,128]{1,0:T(8,128)(2,1)}, u32[]{:S(2)}, u32[]{:S(2)}) collective-permute-start(bf16[512,128]{1,0:T(8,128)(2,1)} %bitcast.67), channel_id=1, source_target_pairs={{0,4},{4,8},{8,12},{12,16},{16,20},{20,24},{24,28},{1,5},{5,9},{9,... | collective-permute-start | bytes 393224 | tf_op jit(solution)/shard_map/ppermute | solution.py:14
  168.2 21.9 %all-to-all-start.1 = ((bf16[128,4,128]{2,0,1:T(8,128)(2,1)}), bf16[128,4,128]{2,0,1:T(8,128)(2,1)}, u32[]{:S(2)}, u32[]{:S(2)}) async-start(bf16[128,4,128]{2,0,1:T(8,128)(2,1)} %copy_bitcast_fusion.3), calls=%async_computation.1 | async-start | bytes 262144 | tf_op jit(solution)/shard_map/all_to_all | solution.py:36
  192.2 41.2 %collective-permute-start = (bf16[512,128]{0,1:T(8,128)(2,1)}, bf16[512,128]{0,1:T(8,128)(2,1)S(1)}, u32[]{:S(2)}, u32[]{:S(2)}) collective-permute-start(bf16[512,128]{0,1:T(8,128)(2,1)} %copy.187), channel_id=1, source_target_pairs={{4,0},{8,4},{12,8},{16,12},{20,16},{24,20},{28,24},{0,28},{5,1},{9... | collective-permute-start | bytes 393224 | tf_op jit(solution)/shard_map/while/body/eval_jaxpr/ppermute | solution.py:20
  212.5 21.0 %collective-permute-start.1 = (bf16[512,128]{1,0:T(8,128)(2,1)}, bf16[512,128]{1,0:T(8,128)(2,1)}, u32[]{:S(2)}, u32[]{:S(2)}) collective-permute-start(bf16[512,128]{1,0:T(8,128)(2,1)} %copy.188), channel_id=1, source_target_pairs={{4,0},{8,4},{12,8},{16,12},{20,16},{24,20},{28,24},{0,28},{5,1},{9... | collective-permute-start | bytes 393224 | tf_op jit(solution)/shard_map/while/body/eval_jaxpr/ppermute | solution.py:20
  254.0 18.1 %collective-permute-start = (bf16[512,128]{0,1:T(8,128)(2,1)}, bf16[512,128]{0,1:T(8,128)(2,1)S(1)}, u32[]{:S(2)}, u32[]{:S(2)}) collective-permute-start(bf16[512,128]{0,1:T(8,128)(2,1)} %copy.187), channel_id=1, source_target_pairs={{4,0},{8,4},{12,8},{16,12},{20,16},{24,20},{28,24},{0,28},{5,1},{9... | collective-permute-start | bytes 393224 | tf_op jit(solution)/shard_map/while/body/eval_jaxpr/ppermute | solution.py:20
  257.5 14.6 %collective-permute-start.1 = (bf16[512,128]{1,0:T(8,128)(2,1)}, bf16[512,128]{1,0:T(8,128)(2,1)}, u32[]{:S(2)}, u32[]{:S(2)}) collective-permute-start(bf16[512,128]{1,0:T(8,128)(2,1)} %copy.188), channel_id=1, source_target_pairs={{4,0},{8,4},{12,8},{16,12},{20,16},{24,20},{28,24},{0,28},{5,1},{9... | collective-permute-start | bytes 393224 | tf_op jit(solution)/shard_map/while/body/eval_jaxpr/ppermute | solution.py:20
  273.5 17.7 %collective-permute-start = (bf16[512,128]{0,1:T(8,128)(2,1)}, bf16[512,128]{0,1:T(8,128)(2,1)S(1)}, u32[]{:S(2)}, u32[]{:S(2)}) collective-permute-start(bf16[512,128]{0,1:T(8,128)(2,1)} %copy.187), channel_id=1, source_target_pairs={{4,0},{8,4},{12,8},{16,12},{20,16},{24,20},{28,24},{0,28},{5,1},{9... | collective-permute-start | bytes 393224 | tf_op jit(solution)/shard_map/while/body/eval_jaxpr/ppermute | solution.py:20
  277.0 14.2 %collective-permute-start.1 = (bf16[512,128]{1,0:T(8,128)(2,1)}, bf16[512,128]{1,0:T(8,128)(2,1)}, u32[]{:S(2)}, u32[]{:S(2)}) collective-permute-start(bf16[512,128]{1,0:T(8,128)(2,1)} %copy.188), channel_id=1, source_target_pairs={{4,0},{8,4},{12,8},{16,12},{20,16},{24,20},{28,24},{0,28},{5,1},{9... | collective-permute-start | bytes 393224 | tf_op jit(solution)/shard_map/while/body/eval_jaxpr/ppermute | solution.py:20
  293.7 27.0 %collective-permute-start = (bf16[512,128]{0,1:T(8,128)(2,1)}, bf16[512,128]{0,1:T(8,128)(2,1)S(1)}, u32[]{:S(2)}, u32[]{:S(2)}) collective-permute-start(bf16[512,128]{0,1:T(8,128)(2,1)} %copy.187), channel_id=1, source_target_pairs={{4,0},{8,4},{12,8},{16,12},{20,16},{24,20},{28,24},{0,28},{5,1},{9... | collective-permute-start | bytes 393224 | tf_op jit(solution)/shard_map/while/body/eval_jaxpr/ppermute | solution.py:20
  297.1 23.5 %collective-permute-start.1 = (bf16[512,128]{1,0:T(8,128)(2,1)}, bf16[512,128]{1,0:T(8,128)(2,1)}, u32[]{:S(2)}, u32[]{:S(2)}) collective-permute-start(bf16[512,128]{1,0:T(8,128)(2,1)} %copy.188), channel_id=1, source_target_pairs={{4,0},{8,4},{12,8},{16,12},{20,16},{24,20},{28,24},{0,28},{5,1},{9... | collective-permute-start | bytes 393224 | tf_op jit(solution)/shard_map/while/body/eval_jaxpr/ppermute | solution.py:20
  302.3 18.3 %collective-permute-start.3 = (f32[512,128]{1,0:T(8,128)}, f32[512,128]{1,0:T(8,128)S(1)}, u32[]{:S(2)}, u32[]{:S(2)}) collective-permute-start(f32[512,128]{1,0:T(8,128)} %add.386), channel_id=1, source_target_pairs={{4,0},{8,4},{12,8},{16,12},{20,16},{24,20},{28,24},{0,28},{5,1},{9... | collective-permute-start | bytes 786440 | tf_op jit(solution)/shard_map/while/body/eval_jaxpr/ppermute | solution.py:20
  323.1 26.1 %collective-permute-start = (bf16[512,128]{0,1:T(8,128)(2,1)}, bf16[512,128]{0,1:T(8,128)(2,1)S(1)}, u32[]{:S(2)}, u32[]{:S(2)}) collective-permute-start(bf16[512,128]{0,1:T(8,128)(2,1)} %copy.187), channel_id=1, source_target_pairs={{4,0},{8,4},{12,8},{16,12},{20,16},{24,20},{28,24},{0,28},{5,1},{9... | collective-permute-start | bytes 393224 | tf_op jit(solution)/shard_map/while/body/eval_jaxpr/ppermute | solution.py:20
  326.6 22.6 %collective-permute-start.1 = (bf16[512,128]{1,0:T(8,128)(2,1)}, bf16[512,128]{1,0:T(8,128)(2,1)}, u32[]{:S(2)}, u32[]{:S(2)}) collective-permute-start(bf16[512,128]{1,0:T(8,128)(2,1)} %copy.188), channel_id=1, source_target_pairs={{4,0},{8,4},{12,8},{16,12},{20,16},{24,20},{28,24},{0,28},{5,1},{9... | collective-permute-start | bytes 393224 | tf_op jit(solution)/shard_map/while/body/eval_jaxpr/ppermute | solution.py:20
  331.8 17.4 %collective-permute-start.3 = (f32[512,128]{1,0:T(8,128)}, f32[512,128]{1,0:T(8,128)S(1)}, u32[]{:S(2)}, u32[]{:S(2)}) collective-permute-start(f32[512,128]{1,0:T(8,128)} %add.386), channel_id=1, source_target_pairs={{4,0},{8,4},{12,8},{16,12},{20,16},{24,20},{28,24},{0,28},{5,1},{9... | collective-permute-start | bytes 786440 | tf_op jit(solution)/shard_map/while/body/eval_jaxpr/ppermute | solution.py:20
  351.7 26.1 %collective-permute-start = (bf16[512,128]{0,1:T(8,128)(2,1)}, bf16[512,128]{0,1:T(8,128)(2,1)S(1)}, u32[]{:S(2)}, u32[]{:S(2)}) collective-permute-start(bf16[512,128]{0,1:T(8,128)(2,1)} %copy.187), channel_id=1, source_target_pairs={{4,0},{8,4},{12,8},{16,12},{20,16},{24,20},{28,24},{0,28},{5,1},{9... | collective-permute-start | bytes 393224 | tf_op jit(solution)/shard_map/while/body/eval_jaxpr/ppermute | solution.py:20
  355.2 22.6 %collective-permute-start.1 = (bf16[512,128]{1,0:T(8,128)(2,1)}, bf16[512,128]{1,0:T(8,128)(2,1)}, u32[]{:S(2)}, u32[]{:S(2)}) collective-permute-start(bf16[512,128]{1,0:T(8,128)(2,1)} %copy.188), channel_id=1, source_target_pairs={{4,0},{8,4},{12,8},{16,12},{20,16},{24,20},{28,24},{0,28},{5,1},{9... | collective-permute-start | bytes 393224 | tf_op jit(solution)/shard_map/while/body/eval_jaxpr/ppermute | solution.py:20
  360.3 17.5 %collective-permute-start.3 = (f32[512,128]{1,0:T(8,128)}, f32[512,128]{1,0:T(8,128)S(1)}, u32[]{:S(2)}, u32[]{:S(2)}) collective-permute-start(f32[512,128]{1,0:T(8,128)} %add.386), channel_id=1, source_target_pairs={{4,0},{8,4},{12,8},{16,12},{20,16},{24,20},{28,24},{0,28},{5,1},{9... | collective-permute-start | bytes 786440 | tf_op jit(solution)/shard_map/while/body/eval_jaxpr/ppermute | solution.py:20
  425.2 27.2 %all-to-all-start.5 = ((bf16[4,128,1024]{2,1,0:T(8,128)(2,1)}), bf16[4,128,1024]{2,1,0:T(8,128)(2,1)S(1)}, u32[]{:S(2)}, u32[]{:S(2)}) async-start(bf16[4,128,1024]{2,1,0:T(8,128)(2,1)} %bitcast.92), calls=%async_computation.5 | async-start | bytes 2097152 | tf_op jit(solution)/shard_map/all_to_all | solution.py:176
  (43 other events, 707.5 us)
where the time goes:
time: 457 us; the launch traced here: 454 us
  starting transfers between devices  118 us (26%)
  waiting for transfers between devices  97.4 us (21%)
  blocking collectives  75.4 us (16%)
  other arithmetic  60.2 us (13%)
  local copies, waits for them, and re-layouts  56.1 us (12%)
  matrix products  30.8 us (7%)
  loops' own time  9.46 us (2%)
  between operations  7.61 us (2%)
    ppermute x30, starting transfers between devices, passed_along(): return lax.ppermute(block, axis, route)  78.3 us
    all_gather x1, blocking collectives, per_device(): all_segments = lax.all_gather(doc_ids, ('blk', 'head'), axis=0, tiled=True)  75.4 us
    all_to_all x1, waiting for transfers between devices, per_device(): lax.all_to_all(output_cotangent, 'head', split_axis=1, concat_axis=0, til...  24.1 us
    add x7, other arithmetic, turn_step(): query_total + query_part  22.4 us
    all_to_all x1, waiting for transfers between devices, per_device(): lax.all_to_all(query_matrix, 'head', split_axis=1, concat_axis=0, tiled=T...  22.1 us
    all_to_all x1, waiting for transfers between devices, per_device(): lax.all_to_all(query_grad, 'head', split_axis=0, concat_axis=1, tiled=True)  21.9 us
    ppermute x30, waiting for transfers between devices, passed_along(): return lax.ppermute(block, axis, route)  17.5 us
    while x28, local copies, waits for them, and re-layouts  15.6 us
  transfers between devices with their start and end apart: 42, of which 15 were waited for; matrix products, arithmetic and copies ran while one was open for 26% of the time, Pallas kernels for 0%

commit v1 on v0

--- a/solution.py
+++ b/solution.py
@@ -6,6 +6,27 @@
 HEAD_WIDTH = 128
 DOC_SPAN = 4
 masked_score = -1e30
+
+
+def _finish_hubs(incoming_x, d0):
+    b_now = list(incoming_x.shape[1:])
+    b_now[d0] *= incoming_x.shape[0]
+    return jnp.moveaxis(incoming_x, 0, d0).reshape(b_now)
+
+
+def solve_patches(vals, shard_axis):
+    k_all = jax.lax.psum(1, axis_name=shard_axis)
+    before = vals[None]
+    for dev_i in range(k_all.bit_length() - 1):
+        x_new = 1 << dev_i
+        g_now = jax.lax.ppermute(
+            before, axis_name=shard_axis, perm=[(tick, tick ^ x_new) for tick in range(k_all)]
+        )
+        x_next = jnp.stack([before, g_now])
+        outcome_arr = jax.lax.axis_index(shard_axis)
+        kept_arr = outcome_arr >> dev_i & 1
+        before = jnp.where(kept_arr == 0, x_next, x_next[::-1]).reshape(-1, *vals.shape)
+    return before
 
 
 def shifted(block, axis, distance):
@@ -35,7 +56,12 @@
         lax.all_to_all(key_matrix, "head", split_axis=1, concat_axis=0, tiled=True),
         lax.all_to_all(value_matrix, "head", split_axis=1, concat_axis=0, tiled=True),
     )
-    all_segments = lax.all_gather(doc_ids, ("blk", "head"), axis=0, tiled=True)
+
+    def post_cells(field, pos_dim, panel):
+        r_now = solve_patches(panel, field)
+        return _finish_hubs(r_now, pos_dim)
+
+    all_segments = post_cells(("blk", "head"), 0, doc_ids)
     my_block = lax.axis_index("blk")
     query_tensor = query_local.reshape(block_rows, kv_heads, heads_per_group, HEAD_WIDTH)
     returned_grads = grad_local.reshape(block_rows, kv_heads, heads_per_group, HEAD_WIDTH)

time: 457 us -> 389 us (0.85)
  blocking collectives: 75.4 us -> 0 us
  starting transfers between devices: 118 us -> 123 us
    all_gather x1 -> x0, blocking collectives: 75.4 us -> none  [per_device(): all_segments = lax.all_gather(doc_ids, ('blk', 'head'), axis=0, tiled=True)]
    ppermute x0 -> x5, waiting for transfers between devices: none -> 24.4 us  [solve_patches(): jax.lax.ppermute(before, axis_name=shard_axis, perm=[(tick, tick ^ x_new)...]
    all_to_all x1, waiting for transfers between devices: 24.1 us -> 0.01 us  [per_device(): lax.all_to_all(output_cotangent, 'head', split_axis=1, concat_axis=0, til...]
    ppermute x0 -> x5, starting transfers between devices: none -> 7.57 us  [solve_patches(): jax.lax.ppermute(before, axis_name=shard_axis, perm=[(tick, tick ^ x_new)...]
  transfers between devices with their start and end apart: 42 -> 47, of which waited for: 15 -> 19; matrix products, arithmetic and copies ran while one was open for 26% -> 31% of each run, Pallas kernels for 0% -> 0%
where the time goes in v1:
time: 389 us; the launch traced here: 386 us
  starting transfers between devices  123 us (32%)
  waiting for transfers between devices  99.1 us (25%)
  other arithmetic  60.2 us (15%)
  local copies, waits for them, and re-layouts  56.2 us (14%)
  matrix products  30.8 us (8%)
  loops' own time  9.43 us (2%)
  between operations  7.41 us (2%)
    ppermute x30, starting transfers between devices, passed_along(): return lax.ppermute(block, axis, route)  77.6 us
    ppermute x5, waiting for transfers between devices, solve_patches(): jax.lax.ppermute(before, axis_name=shard_axis, perm=[(tick, tick ^ x_new)...  24.4 us
    add x7, other arithmetic, turn_step(): query_total + query_part  22.5 us
    all_to_all x1, waiting for transfers between devices, per_device(): lax.all_to_all(query_matrix, 'head', split_axis=1, concat_axis=0, tiled=T...  22.1 us
    all_to_all x1, waiting for transfers between devices, per_device(): lax.all_to_all(query_grad, 'head', split_axis=0, concat_axis=1, tiled=True)  21.9 us
    ppermute x30, waiting for transfers between devices, passed_along(): return lax.ppermute(block, axis, route)  17.4 us
    while x28, local copies, waits for them, and re-layouts  15.6 us
    add x7, other arithmetic, turn_step(): summed_key_grad + key_part  12.3 us
  transfers between devices with their start and end apart: 47, of which 19 were waited for; matrix products, arithmetic and copies ran while one was open for 31% of the time, Pallas kernels for 0%

profile of v1, /device:TPU:6, one launch (start us, length us, event | category | flops | bytes accessed | tf_op | source)
XLA Modules:
  0.0 385.9 jit_solution(15656317097572810317)
XLA Ops:
  2.2 4.9 %all-to-all-start = ((bf16[128,4,128]{2,0,1:T(8,128)(2,1)}), bf16[128,4,128]{2,0,1:T(8,128)(2,1)}, u32[]{:S(2)}, u32[]{:S(2)}) async-start(bf16[128,4,128]{2,0,1:T(8,128)(2,1)} %copy_bitcast_fusion.4), calls=%async_computation | async-start | bytes 262144 | tf_op jit(solution)/shard_map/all_to_all | solution.py:56
  9.4 3.9 %all-to-all-done = bf16[128,4,128]{2,0,1:T(8,128)(2,1)} async-done(((bf16[128,4,128]{2,0,1:T(8,128)(2,1)}), bf16[128,4,128]{2,0,1:T(8,128)(2,1)}, u32[]{:S(2)}, u32[]{:S(2)}) %all-to-all-start) | async-done | bytes 131104 | tf_op jit(solution)/shard_map/all_to_all | solution.py:56
  13.3 3.5 all-to-all-start.2
  19.1 22.1 %all-to-all-done.2 = bf16[128,4,1024]{2,0,1:T(8,128)(2,1)S(1)} async-done(((bf16[128,4,1024]{2,0,1:T(8,128)(2,1)}), bf16[128,4,1024]{2,0,1:T(8,128)(2,1)S(1)}, u32[]{:S(2)}, u32[]{:S(2)}) %all-to-all-start.2) | async-done | bytes 1048608 | tf_op jit(solution)/shard_map/all_to_all | solution.py:53
  46.7 14.6 %collective-permute-done.4 = s32[1,128]{1,0:T(1,128)S(1)} collective-permute-done((s32[1,128]{1,0:T(1,128)S(1)}, s32[1,128]{1,0:T(1,128)S(1)}, u32[]{:S(2)}, u32[]{:S(2)}) %collective-permute-start.4) | collective-permute-done | bytes 544 | tf_op jit(solution)/shard_map/ppermute | solution.py:22
  61.4 4.5 %collective-permute-start.5 = (s32[2,128]{1,0:T(2,128)S(1)}, s32[2,128]{1,0:T(2,128)S(1)}, u32[]{:S(2)}, u32[]{:S(2)}) collective-permute-start(s32[2,128]{1,0:T(2,128)S(1)} %bitcast.390), channel_id=1, source_target_pairs={{0,2},{1,3},{2,0},{3,1},{4,6},{5,7},{6,4},{7,5},{8,10},{9,11},{10,... | collective-permute-start | bytes 3080 | tf_op jit(solution)/shard_map/ppermute | solution.py:22
  65.9 4.1 %collective-permute-done.5 = s32[2,128]{1,0:T(2,128)S(1)} collective-permute-done((s32[2,128]{1,0:T(2,128)S(1)}, s32[2,128]{1,0:T(2,128)S(1)}, u32[]{:S(2)}, u32[]{:S(2)}) %collective-permute-start.5) | collective-permute-done | bytes 1056 | tf_op jit(solution)/shard_map/ppermute | solution.py:22
  71.2 4.3 %all-to-all-start.4 = ((bf16[128,4,1024]{2,0,1:T(8,128)(2,1)}), bf16[128,4,1024]{2,0,1:T(8,128)(2,1)}, u32[]{:S(2)}, u32[]{:S(2)}) async-start(bf16[128,4,1024]{2,0,1:T(8,128)(2,1)} %bitcast.340), calls=%async_computation.4 | async-start | bytes 2097152 | tf_op jit(solution)/shard_map/all_to_all | solution.py:55
  102.1 3.9 %all-to-all-start.1 = ((bf16[128,4,128]{2,0,1:T(8,128)(2,1)}), bf16[128,4,128]{2,0,1:T(8,128)(2,1)}, u32[]{:S(2)}, u32[]{:S(2)}) async-start(bf16[128,4,128]{2,0,1:T(8,128)(2,1)} %copy_bitcast_fusion.3), calls=%async_computation.1 | async-start | bytes 262144 | tf_op jit(solution)/shard_map/all_to_all | solution.py:57
  115.7 5.7 %conditional.6 = ((f32[1,8,512,1]{2,1,3,0:T(8,128)S(1)}, f32[1,8,512,1]{2,1,3,0:T(8,128)S(1)})) conditional(s32[]{:T(128)} %convert_element_type.80, (f32[1,8,512,1]{2,1,3,0:T(8,128)S(1)}, f32[1,8,512,1]{2,1,3,0:T(8,128)S(1)}) %tuple.89, (s32[512]{0:T(512)S(1)}, s32[]{:T(128)}, s32[4096]{0:T(1024)}, s32[512]{0:T(512)S(1)}, ...), branch_computations={%region_2.3_spmd, %region_3.6_spmd} | conditional | flops 554443264 | bytes 18970726 | solution.py:116
  123.9 187.3 %while.26 = (s32[]{:T(128)}, bf16[512,128]{0,1:T(8,128)(2,1)S(1)}, bf16[512,128]{1,0:T(8,128)(2,1)}, f32[512,1024]{0,1:T(8,128)}, f32[512,128]{1,0:T(8,128)}, /*...) while((s32[]{:T(128)}, bf16[512,128]{0,1:T(8,128)(2,1)S(1)}, ...), condition=%wide.region_22.23_spmd.clone, body=%wide.region_19.22_spmd.clone.sunk | while | flops 2711487488 | bytes 62722972 | solution.py:189
  124.5 17.9 %collective-permute-start = (bf16[512,128]{0,1:T(8,128)(2,1)}, bf16[512,128]{0,1:T(8,128)(2,1)S(1)}, u32[]{:S(2)}, u32[]{:S(2)}) collective-permute-start(bf16[512,128]{0,1:T(8,128)(2,1)} %copy.187), channel_id=1, source_target_pairs={{4,0},{8,4},{12,8},{16,12},{20,16},{24,20},{28,24},{0,28},{5,1},{9... | collective-permute-start | bytes 393224 | tf_op jit(solution)/shard_map/while/body/eval_jaxpr/ppermute | solution.py:41
  146.4 13.3 %conditional.13 = (f32[512,1024]{0,1:T(8,128)S(1)}, f32[512,128]{1,0:T(8,128)}, f32[512,128]{1,0:T(8,128)S(1)}) conditional(s32[]{:T(128)} %convert_element_type.114, () %tuple.153, (s32[512]{0:T(512)S(1)}, s32[]{:T(128)}, s32[4096]{0:T(1024)}, s32[]{:T(128)}, bf16[512,1,8,128]{3,0,2,1:T(8,128)(2,1)S(1)}, /*index=5*/bf16[512,128]{0,1:T(8,128)(2,1)}, ...), branch_computations={%region_20.20_spmd, %region_21.21_spmd} | conditional | flops 2710307840 | bytes 50137280 | solution.py:159
  151.9 4.2 %fusion.29 = bf16[8,512,512]{1,2,0:T(8,128)(2,1)S(1)} fusion(f32[512,512,8]{1,0,2:T(8,128)S(1)} %fusion.39, f32[8,512]{1,0:T(8,128)S(1)} %bitcast.379, f32[8,512]{1,0:T(8,128)S(1)} %bitcast.381, pred[512,512]{0,1:T(8,128)(4,1)S(1)} %compare_and_fusion.4, bf16[512,1,8,128]{3,0,2,1:T(8,128)(2,1)S(1)} %copy-done.11, bf16[512,128]{1,0:T(8,128)(2,1)} %get-tuple-element.614), kind=kOutput, calls=%fused_computation.54 | convolution fusion | flops 551550976 | bytes 14057472 | tf_op jit(solution)/shard_map/while/body/eval_jaxpr/cond/branch_1_fun/ighd,jgd->ghij/dot_general | solution.py:131
  233.8 13.2 %collective-permute-start.3 = (f32[512,128]{1,0:T(8,128)}, f32[512,128]{1,0:T(8,128)S(1)}, u32[]{:S(2)}, u32[]{:S(2)}) collective-permute-start(f32[512,128]{1,0:T(8,128)} %add.404), channel_id=1, source_target_pairs={{4,0},{8,4},{12,8},{16,12},{20,16},{24,20},{28,24},{0,28},{5,1},{9... | collective-permute-start | bytes 786440 | tf_op jit(solution)/shard_map/while/body/eval_jaxpr/ppermute | solution.py:41
  263.3 12.3 %collective-permute-start.3 = (f32[512,128]{1,0:T(8,128)}, f32[512,128]{1,0:T(8,128)S(1)}, u32[]{:S(2)}, u32[]{:S(2)}) collective-permute-start(f32[512,128]{1,0:T(8,128)} %add.404), channel_id=1, source_target_pairs={{4,0},{8,4},{12,8},{16,12},{20,16},{24,20},{28,24},{0,28},{5,1},{9... | collective-permute-start | bytes 786440 | tf_op jit(solution)/shard_map/while/body/eval_jaxpr/ppermute | solution.py:41
  291.9 12.3 %collective-permute-start.3 = (f32[512,128]{1,0:T(8,128)}, f32[512,128]{1,0:T(8,128)S(1)}, u32[]{:S(2)}, u32[]{:S(2)}) collective-permute-start(f32[512,128]{1,0:T(8,128)} %add.404), channel_id=1, source_target_pairs={{4,0},{8,4},{12,8},{16,12},{20,16},{24,20},{28,24},{0,28},{5,1},{9... | collective-permute-start | bytes 786440 | tf_op jit(solution)/shard_map/while/body/eval_jaxpr/ppermute | solution.py:41
  311.1 16.7 %conditional.10 = (f32[512,1024]{0,1:T(8,128)}, f32[512,128]{1,0:T(8,128)}, f32[512,128]{1,0:T(8,128)}) conditional(s32[]{:T(128)} %convert_element_type.85, () %tuple.95, (s32[512]{0:T(512)S(1)}, s32[]{:T(128)}, s32[4096]{0:T(1024)}, s32[512]{0:T(512)S(1)}, bf16[512,1,8,128]{3,2,0,1:T(8,128)(2,1)}, /*index=5*/bf16[512,128]{0,1:T(8,128)(2,1)S(1)}, ...), branch_computations={%region_23.24_spmd, %region_24.25_spmd} | conditional | flops 2710307328 | bytes 54360276 | solution.py:159
  319.4 4.4 %fusion.55 = bf16[8,512,512]{1,2,0:T(8,128)(2,1)S(1)} fusion(f32[512,512,8]{1,0,2:T(8,128)S(1)} %fusion.65, f32[8,512]{1,0:T(8,128)S(1)} %bitcast.384, f32[8,512]{1,0:T(8,128)S(1)} %bitcast.383, pred[512,512]{0,1:T(8,128)(4,1)S(1)} %compare_and_fusion.5, bf16[512,1,8,128]{3,2,0,1:T(8,128)(2,1)S(1)} %copy-done.8, bf16[512,128]{1,0:T(8,128)(2,1)} %get-tuple-element.643), kind=kOutput, calls=%fused_computation.83 | convolution fusion | flops 551550976 | bytes 14057472 | tf_op jit(solution)/shard_map/cond/branch_1_fun/ighd,jgd->ghij/dot_general | solution.py:131
  332.3 4.2 %collective-permute-done.14 = bf16[512,128]{1,0:T(8,128)(2,1)} collective-permute-done((bf16[512,128]{1,0:T(8,128)(2,1)S(1)}, bf16[512,128]{1,0:T(8,128)(2,1)}, u32[]{:S(2)}, u32[]{:S(2)}) %collective-permute-start.14) | collective-permute-done | bytes 131104 | tf_op jit(solution)/shard_map/ppermute | solution.py:41
  336.5 4.8 %all-to-all-start.7 = ((bf16[4,128,128]{2,1,0:T(8,128)(2,1)}), bf16[4,128,128]{2,1,0:T(8,128)(2,1)S(1)}, u32[]{:S(2)}, u32[]{:S(2)}) async-start(bf16[4,128,128]{2,1,0:T(8,128)(2,1)} %bitcast.112), calls=%async_computation.7 | async-start | bytes 262144 | tf_op jit(solution)/shard_map/all_to_all | solution.py:204
  342.0 5.5 %all-to-all-done.7 = bf16[4,128,128]{2,1,0:T(8,128)(2,1)S(1)} async-done(((bf16[4,128,128]{2,1,0:T(8,128)(2,1)}), bf16[4,128,128]{2,1,0:T(8,128)(2,1)S(1)}, u32[]{:S(2)}, u32[]{:S(2)}) %all-to-all-start.7) | async-done | bytes 131104 | tf_op jit(solution)/shard_map/all_to_all | solution.py:204
  356.7 3.5 all-to-all-start.5
  362.1 21.9 %all-to-all-done.5 = bf16[4,128,1024]{2,1,0:T(8,128)(2,1)S(1)} async-done(((bf16[4,128,1024]{2,1,0:T(8,128)(2,1)}), bf16[4,128,1024]{2,1,0:T(8,128)(2,1)S(1)}, u32[]{:S(2)}, u32[]{:S(2)}) %all-to-all-start.5) | async-done | bytes 1048608 | tf_op jit(solution)/shard_map/all_to_all | solution.py:202
  (272 shorter events, 205.7 us)
Async XLA Ops:
  13.3 28.0 %all-to-all-start.2 = ((bf16[128,4,1024]{2,0,1:T(8,128)(2,1)}), bf16[128,4,1024]{2,0,1:T(8,128)(2,1)S(1)}, u32[]{:S(2)}, u32[]{:S(2)}) async-start(bf16[128,4,1024]{2,0,1:T(8,128)(2,1)} %bitcast.342), calls=%async_computation.2 | async-start | bytes 2097152 | tf_op jit(solution)/shard_map/all_to_all | solution.py:53
  41.2 30.0 %all-to-all-start.3 = ((bf16[128,4,1024]{2,0,1:T(8,128)(2,1)}), bf16[128,4,1024]{2,0,1:T(8,128)(2,1)S(1)}, u32[]{:S(2)}, u32[]{:S(2)}) async-start(bf16[128,4,1024]{2,0,1:T(8,128)(2,1)} %bitcast.341), calls=%async_computation.3 | async-start | bytes 2097152 | tf_op jit(solution)/shard_map/all_to_all | solution.py:54
  44.8 16.6 %collective-permute-start.4 = (s32[1,128]{1,0:T(1,128)S(1)}, s32[1,128]{1,0:T(1,128)S(1)}, u32[]{:S(2)}, u32[]{:S(2)}) collective-permute-start(s32[1,128]{1,0:T(1,128)S(1)} %bitcast.395), channel_id=1, source_target_pairs={{0,1},{1,0},{2,3},{3,2},{4,5},{5,4},{6,7},{7,6},{8,9},{9,8},{10,11... | collective-permute-start | bytes 1544 | tf_op jit(solution)/shard_map/ppermute | solution.py:22
  71.2 31.0 %all-to-all-start.4 = ((bf16[128,4,1024]{2,0,1:T(8,128)(2,1)}), bf16[128,4,1024]{2,0,1:T(8,128)(2,1)}, u32[]{:S(2)}, u32[]{:S(2)}) async-start(bf16[128,4,1024]{2,0,1:T(8,128)(2,1)} %bitcast.340), calls=%async_computation.4 | async-start | bytes 2097152 | tf_op jit(solution)/shard_map/all_to_all | solution.py:55
  91.3 30.3 %collective-permute-start.12 = (bf16[512,128]{1,0:T(8,128)(2,1)}, bf16[512,128]{1,0:T(8,128)(2,1)}, u32[]{:S(2)}, u32[]{:S(2)}) collective-permute-start(bf16[512,128]{1,0:T(8,128)(2,1)} %bitcast.67), channel_id=1, source_target_pairs={{0,16},{4,20},{8,24},{12,28},{1,17},{5,21},{9,25},{13,29},{2,18},{... | collective-permute-start | bytes 393224 | tf_op jit(solution)/shard_map/ppermute | solution.py:35
  92.6 28.9 %collective-permute-start.11 = (bf16[512,128]{1,0:T(8,128)(2,1)}, bf16[512,128]{1,0:T(8,128)(2,1)}, u32[]{:S(2)}, u32[]{:S(2)}) collective-permute-start(bf16[512,128]{1,0:T(8,128)(2,1)} %bitcast.67), channel_id=1, source_target_pairs={{0,12},{4,16},{8,20},{12,24},{16,28},{1,13},{5,17},{9,21},{13,25},... | collective-permute-start | bytes 393224 | tf_op jit(solution)/shard_map/ppermute | solution.py:35
  93.9 27.4 %collective-permute-start.10 = (bf16[512,128]{1,0:T(8,128)(2,1)}, bf16[512,128]{1,0:T(8,128)(2,1)}, u32[]{:S(2)}, u32[]{:S(2)}) collective-permute-start(bf16[512,128]{1,0:T(8,128)(2,1)} %bitcast.67), channel_id=1, source_target_pairs={{0,8},{4,12},{8,16},{12,20},{16,24},{20,28},{1,9},{5,13},{9,17},{1... | collective-permute-start | bytes 393224 | tf_op jit(solution)/shard_map/ppermute | solution.py:35
  95.2 20.5 %collective-permute-start.9 = (bf16[512,128]{1,0:T(8,128)(2,1)}, bf16[512,128]{1,0:T(8,128)(2,1)}, u32[]{:S(2)}, u32[]{:S(2)}) collective-permute-start(bf16[512,128]{1,0:T(8,128)(2,1)} %bitcast.67), channel_id=1, source_target_pairs={{0,4},{4,8},{8,12},{12,16},{16,20},{20,24},{24,28},{1,5},{5,9},{9,... | collective-permute-start | bytes 393224 | tf_op jit(solution)/shard_map/ppermute | solution.py:35
  102.1 20.3 %all-to-all-start.1 = ((bf16[128,4,128]{2,0,1:T(8,128)(2,1)}), bf16[128,4,128]{2,0,1:T(8,128)(2,1)}, u32[]{:S(2)}, u32[]{:S(2)}) async-start(bf16[128,4,128]{2,0,1:T(8,128)(2,1)} %copy_bitcast_fusion.3), calls=%async_computation.1 | async-start | bytes 262144 | tf_op jit(solution)/shard_map/all_to_all | solution.py:57
  124.5 40.5 %collective-permute-start = (bf16[512,128]{0,1:T(8,128)(2,1)}, bf16[512,128]{0,1:T(8,128)(2,1)S(1)}, u32[]{:S(2)}, u32[]{:S(2)}) collective-permute-start(bf16[512,128]{0,1:T(8,128)(2,1)} %copy.187), channel_id=1, source_target_pairs={{4,0},{8,4},{12,8},{16,12},{20,16},{24,20},{28,24},{0,28},{5,1},{9... | collective-permute-start | bytes 393224 | tf_op jit(solution)/shard_map/while/body/eval_jaxpr/ppermute | solution.py:41
  144.0 21.0 %collective-permute-start.1 = (bf16[512,128]{1,0:T(8,128)(2,1)}, bf16[512,128]{1,0:T(8,128)(2,1)}, u32[]{:S(2)}, u32[]{:S(2)}) collective-permute-start(bf16[512,128]{1,0:T(8,128)(2,1)} %copy.188), channel_id=1, source_target_pairs={{4,0},{8,4},{12,8},{16,12},{20,16},{24,20},{28,24},{0,28},{5,1},{9... | collective-permute-start | bytes 393224 | tf_op jit(solution)/shard_map/while/body/eval_jaxpr/ppermute | solution.py:41
  185.4 18.2 %collective-permute-start = (bf16[512,128]{0,1:T(8,128)(2,1)}, bf16[512,128]{0,1:T(8,128)(2,1)S(1)}, u32[]{:S(2)}, u32[]{:S(2)}) collective-permute-start(bf16[512,128]{0,1:T(8,128)(2,1)} %copy.187), channel_id=1, source_target_pairs={{4,0},{8,4},{12,8},{16,12},{20,16},{24,20},{28,24},{0,28},{5,1},{9... | collective-permute-start | bytes 393224 | tf_op jit(solution)/shard_map/while/body/eval_jaxpr/ppermute | solution.py:41
  188.8 14.8 %collective-permute-start.1 = (bf16[512,128]{1,0:T(8,128)(2,1)}, bf16[512,128]{1,0:T(8,128)(2,1)}, u32[]{:S(2)}, u32[]{:S(2)}) collective-permute-start(bf16[512,128]{1,0:T(8,128)(2,1)} %copy.188), channel_id=1, source_target_pairs={{4,0},{8,4},{12,8},{16,12},{20,16},{24,20},{28,24},{0,28},{5,1},{9... | collective-permute-start | bytes 393224 | tf_op jit(solution)/shard_map/while/body/eval_jaxpr/ppermute | solution.py:41
  205.0 17.7 %collective-permute-start = (bf16[512,128]{0,1:T(8,128)(2,1)}, bf16[512,128]{0,1:T(8,128)(2,1)S(1)}, u32[]{:S(2)}, u32[]{:S(2)}) collective-permute-start(bf16[512,128]{0,1:T(8,128)(2,1)} %copy.187), channel_id=1, source_target_pairs={{4,0},{8,4},{12,8},{16,12},{20,16},{24,20},{28,24},{0,28},{5,1},{9... | collective-permute-start | bytes 393224 | tf_op jit(solution)/shard_map/while/body/eval_jaxpr/ppermute | solution.py:41
  225.2 27.0 %collective-permute-start = (bf16[512,128]{0,1:T(8,128)(2,1)}, bf16[512,128]{0,1:T(8,128)(2,1)S(1)}, u32[]{:S(2)}, u32[]{:S(2)}) collective-permute-start(bf16[512,128]{0,1:T(8,128)(2,1)} %copy.187), channel_id=1, source_target_pairs={{4,0},{8,4},{12,8},{16,12},{20,16},{24,20},{28,24},{0,28},{5,1},{9... | collective-permute-start | bytes 393224 | tf_op jit(solution)/shard_map/while/body/eval_jaxpr/ppermute | solution.py:41
  228.7 23.5 %collective-permute-start.1 = (bf16[512,128]{1,0:T(8,128)(2,1)}, bf16[512,128]{1,0:T(8,128)(2,1)}, u32[]{:S(2)}, u32[]{:S(2)}) collective-permute-start(bf16[512,128]{1,0:T(8,128)(2,1)} %copy.188), channel_id=1, source_target_pairs={{4,0},{8,4},{12,8},{16,12},{20,16},{24,20},{28,24},{0,28},{5,1},{9... | collective-permute-start | bytes 393224 | tf_op jit(solution)/shard_map/while/body/eval_jaxpr/ppermute | solution.py:41
  233.8 18.4 %collective-permute-start.3 = (f32[512,128]{1,0:T(8,128)}, f32[512,128]{1,0:T(8,128)S(1)}, u32[]{:S(2)}, u32[]{:S(2)}) collective-permute-start(f32[512,128]{1,0:T(8,128)} %add.404), channel_id=1, source_target_pairs={{4,0},{8,4},{12,8},{16,12},{20,16},{24,20},{28,24},{0,28},{5,1},{9... | collective-permute-start | bytes 786440 | tf_op jit(solution)/shard_map/while/body/eval_jaxpr/ppermute | solution.py:41
  254.7 26.1 %collective-permute-start = (bf16[512,128]{0,1:T(8,128)(2,1)}, bf16[512,128]{0,1:T(8,128)(2,1)S(1)}, u32[]{:S(2)}, u32[]{:S(2)}) collective-permute-start(bf16[512,128]{0,1:T(8,128)(2,1)} %copy.187), channel_id=1, source_target_pairs={{4,0},{8,4},{12,8},{16,12},{20,16},{24,20},{28,24},{0,28},{5,1},{9... | collective-permute-start | bytes 393224 | tf_op jit(solution)/shard_map/while/body/eval_jaxpr/ppermute | solution.py:41
  258.1 22.6 %collective-permute-start.1 = (bf16[512,128]{1,0:T(8,128)(2,1)}, bf16[512,128]{1,0:T(8,128)(2,1)}, u32[]{:S(2)}, u32[]{:S(2)}) collective-permute-start(bf16[512,128]{1,0:T(8,128)(2,1)} %copy.188), channel_id=1, source_target_pairs={{4,0},{8,4},{12,8},{16,12},{20,16},{24,20},{28,24},{0,28},{5,1},{9... | collective-permute-start | bytes 393224 | tf_op jit(solution)/shard_map/while/body/eval_jaxpr/ppermute | solution.py:41
  263.3 17.5 %collective-permute-start.3 = (f32[512,128]{1,0:T(8,128)}, f32[512,128]{1,0:T(8,128)S(1)}, u32[]{:S(2)}, u32[]{:S(2)}) collective-permute-start(f32[512,128]{1,0:T(8,128)} %add.404), channel_id=1, source_target_pairs={{4,0},{8,4},{12,8},{16,12},{20,16},{24,20},{28,24},{0,28},{5,1},{9... | collective-permute-start | bytes 786440 | tf_op jit(solution)/shard_map/while/body/eval_jaxpr/ppermute | solution.py:41
  283.2 26.1 %collective-permute-start = (bf16[512,128]{0,1:T(8,128)(2,1)}, bf16[512,128]{0,1:T(8,128)(2,1)S(1)}, u32[]{:S(2)}, u32[]{:S(2)}) collective-permute-start(bf16[512,128]{0,1:T(8,128)(2,1)} %copy.187), channel_id=1, source_target_pairs={{4,0},{8,4},{12,8},{16,12},{20,16},{24,20},{28,24},{0,28},{5,1},{9... | collective-permute-start | bytes 393224 | tf_op jit(solution)/shard_map/while/body/eval_jaxpr/ppermute | solution.py:41
  286.7 22.6 %collective-permute-start.1 = (bf16[512,128]{1,0:T(8,128)(2,1)}, bf16[512,128]{1,0:T(8,128)(2,1)}, u32[]{:S(2)}, u32[]{:S(2)}) collective-permute-start(bf16[512,128]{1,0:T(8,128)(2,1)} %copy.188), channel_id=1, source_target_pairs={{4,0},{8,4},{12,8},{16,12},{20,16},{24,20},{28,24},{0,28},{5,1},{9... | collective-permute-start | bytes 393224 | tf_op jit(solution)/shard_map/while/body/eval_jaxpr/ppermute | solution.py:41
  291.9 17.5 %collective-permute-start.3 = (f32[512,128]{1,0:T(8,128)}, f32[512,128]{1,0:T(8,128)S(1)}, u32[]{:S(2)}, u32[]{:S(2)}) collective-permute-start(f32[512,128]{1,0:T(8,128)} %add.404), channel_id=1, source_target_pairs={{4,0},{8,4},{12,8},{16,12},{20,16},{24,20},{28,24},{0,28},{5,1},{9... | collective-permute-start | bytes 786440 | tf_op jit(solution)/shard_map/while/body/eval_jaxpr/ppermute | solution.py:41
  356.7 27.2 %all-to-all-start.5 = ((bf16[4,128,1024]{2,1,0:T(8,128)(2,1)}), bf16[4,128,1024]{2,1,0:T(8,128)(2,1)S(1)}, u32[]{:S(2)}, u32[]{:S(2)}) async-start(bf16[4,128,1024]{2,1,0:T(8,128)(2,1)} %bitcast.106), calls=%async_computation.5 | async-start | bytes 2097152 | tf_op jit(solution)/shard_map/all_to_all | solution.py:202
  (48 other events, 583.3 us)
